TPU v7x, 128 devices: a whole 4x4x4 slice. The times are simulated.
128 devices in a mesh: shard: 32 (over x, y, core), tensor: 4 (over z).
Axes of the slice: x: 4, y: 4, z: 4, core: 2. Of those that a mesh axis runs over, the one named last changes fastest.
Arguments:
- grads: bfloat16 [384, 256, 256], P('shard', 'tensor'), may hold values from -60 to 60
- owner: int32 [384], replicated, may hold values from 0 to 31, as said below
- slot: int32 [384], replicated, may hold values from 0 to 23, as said below
- stat_left: float32 [768, 256, 256], P('shard', 'tensor'), may hold values from -144 to 2704, as said below
- stat_right: float32 [768, 256, 256], P('shard', 'tensor'), may hold values from -144 to 2704, as said below
- root_left: float32 [768, 256, 256], P('shard', 'tensor'), may hold values from -0.72 to 2.72, as said below
- root_right: float32 [768, 256, 256], P('shard'), may hold values from -0.72 to 2.72, as said below
- moment: float32 [768, 256, 256], P('shard', 'tensor'), may hold values from 0.1 to 10
- momentum: float32 [768, 256, 256], P('shard', 'tensor'), may hold values from -6 to 6
- master: float32 [768, 256, 256], P('shard', 'tensor'), may hold values from -0.3 to 0.3
Outputs:
- stat_left_new: float32 [768, 256, 256], P('shard', 'tensor')
- stat_right_new: float32 [768, 256, 256], P('shard', 'tensor')
- moment_new: float32 [768, 256, 256], P('shard', 'tensor')
- momentum_new: float32 [768, 256, 256], P('shard', 'tensor')
- master_new: float32 [768, 256, 256], P('shard', 'tensor')
- weights_new: bfloat16 [384, 256, 256], P('shard', 'tensor')
Inputs may be any that keep to these rules, and one draw needn't show every extreme that they name: Each owner group holds at most 24 blocks, some exactly 24; no owner group holds two blocks of one shard group (blocks b with equal b // 12). `slot`: the blocks of one owner group have distinct slots. `stat_left`: Symmetric. `stat_right`: Symmetric. `root_left`: Symmetric. `root_right`: Symmetric.
All inputs are finite; a program needn't handle non-finite values.
Results may differ from a plain program's by a relative error of at most 0.001.
Values may be sent and summed in bfloat16 or wider, within the bound.
No kernel may reach another device: no remote copies, remote signals or barrier semaphores. Data moves between devices by JAX's collectives and lax.ppermute only.
A program may use at most 128 MiB of HBM per device.

v0:
```python
import jax
import jax.numpy as jnp
from jax import lax
from jax.sharding import PartitionSpec as P

beta_stat = 0.95
beta_mom = 0.9
learn_rate = 0.01
eps_root = 1e-08
eps_mean = 1e-06


def on_device(
    grads, owner, slot, stat_left, stat_right, root_left, root_right, moment, momentum, master
):
    groups = lax.axis_size("shard")
    splits = lax.axis_size("tensor")
    slots_dev = stat_left.shape[0]
    rows_dev = stat_left.shape[1]
    order = stat_left.shape[2]
    blocks_group = grads.shape[0]
    shard_index = lax.axis_index("shard")
    tensor_index = lax.axis_index("tensor")
    owner_grid = owner.reshape(groups, blocks_group)
    slot_grid = slot.reshape(groups, blocks_group)
    local_owner = lax.dynamic_index_in_dim(owner_grid, shard_index, 0, keepdims=False)
    hit_mask = owner_grid == shard_index
    slot_ids = jnp.arange(slots_dev, dtype=jnp.int32)
    select = jnp.sum(
        (slot_grid[None, :, :] == slot_ids[:, None, None]) & hit_mask[None, :, :], axis=2
    ).astype(jnp.bfloat16)
    group_ids = jnp.arange(groups, dtype=jnp.int32)
    picker = (local_owner[None, :] == group_ids[:, None]).astype(jnp.bfloat16)
    row_start = tensor_index * rows_dev
    whole_rows = lax.all_gather(grads, "tensor", axis=1, tiled=True)
    outgoing = jnp.einsum(
        "gi,ixy->gxy", picker, whole_rows, preferred_element_type=jnp.float32
    ).astype(jnp.bfloat16)
    arrived = lax.all_to_all(outgoing, "shard", split_axis=0, concat_axis=0, tiled=True)
    grad_whole = jnp.einsum(
        "kg,gxy->kxy", select, arrived, preferred_element_type=jnp.float32
    ).astype(jnp.bfloat16)
    grad_piece = lax.dynamic_slice_in_dim(grad_whole, row_start, rows_dev, 1)
    highest = lax.Precision.HIGHEST
    grad_full = grad_whole.astype(jnp.float32)
    grad_rows = grad_piece.astype(jnp.float32)
    grad_cols = lax.dynamic_slice_in_dim(grad_full, row_start, rows_dev, 2)
    left_new = beta_stat * stat_left + (1.0 - beta_stat) * jnp.einsum(
        "kij,klj->kil", grad_rows, grad_full, precision=highest
    )
    right_new = beta_stat * stat_right + (1.0 - beta_stat) * jnp.einsum(
        "kji,kjl->kil", grad_cols, grad_full, precision=highest
    )
    second_new = beta_stat * moment + (1.0 - beta_stat) * grad_rows * grad_rows
    adam_step = grad_rows / (jnp.sqrt(second_new) + eps_root)
    precond = jnp.einsum("kij,kjl->kil", root_left, grad_full, precision=highest)
    precond = jnp.einsum("kij,kjl->kil", precond, root_right, precision=highest)
    adam_sum, precond_sum = lax.psum(
        (jnp.sum(adam_step * adam_step, axis=(1, 2)), jnp.sum(precond * precond, axis=(1, 2))),
        "tensor",
    )
    entries = float(rows_dev * splits * order)
    scale_ratio = jnp.sqrt(adam_sum / entries + eps_mean) / jnp.sqrt(
        precond_sum / entries + eps_mean
    )
    velocity_new = beta_mom * momentum + (1.0 - beta_mom) * scale_ratio[:, None, None] * precond
    weight_new = master - learn_rate * velocity_new
    weight_half = weight_new.astype(jnp.bfloat16)
    returning = jnp.einsum(
        "kg,kxy->gxy", select, weight_half, preferred_element_type=jnp.float32
    ).astype(jnp.bfloat16)
    back_rows = lax.all_to_all(returning, "shard", split_axis=0, concat_axis=0, tiled=True)
    weights_local = jnp.take(back_rows, local_owner, axis=0)
    return (left_new, right_new, second_new, velocity_new, weight_new, weights_local)


def solution(mesh):
    placed = (
        P("shard", "tensor", None),
        P(),
        P(),
        P("shard", "tensor", None),
        P("shard", "tensor", None),
        P("shard", "tensor", None),
        P("shard", None, None),
        P("shard", "tensor", None),
        P("shard", "tensor", None),
        P("shard", "tensor", None),
    )
    return jax.shard_map(
        on_device,
        mesh=mesh,
        in_specs=placed,
        out_specs=(
            P("shard", "tensor", None),
            P("shard", "tensor", None),
            P("shard", "tensor", None),
            P("shard", "tensor", None),
            P("shard", "tensor", None),
            P("shard", "tensor", None),
        ),
        check_vma=False,
    )
```

profile of v0, /device:TPU:1, one launch (start us, length us, event | category | flops | bytes accessed | tf_op | source)
XLA Modules:
  0.0 176.2 jit_solution(17148994907368642026)
XLA Ops:
  7.2 0.7 all-gather.2.cloned.1.call-update
  7.9 0.8 reshape.57
  8.7 30.7 %all-gather.2.cloned.1.call-done = bf16[12,256,256]{2,1,0:T(8,128)(2,1)} async-done(((bf16[12,64,256]{2,1,0:T(8,128)(2,1)}), bf16[12,256,256]{2,1,0:T(8,128)(2,1)}) %all-gather.2.cloned.1.call-update) | async-done | bytes 1572880 | tf_op jit(solution)/shard_map/all_gather | solution.py:35
  39.4 2.8 %convolution_convert_fusion = bf16[32,256,256]{2,0,1:T(8,128)(2,1)S(1)} fusion(bf16[12,256,256]{2,1,0:T(8,128)(2,1)} %all-gather.2.cloned.1.call-done, s32[12]{0:T(128)S(1)} %get-tuple-element.39), kind=kOutput, calls=%fused_computation.3 | convolution fusion | flops 52429184 | bytes 5767216 | tf_op jit(solution)/shard_map/gi,ixy->gxy/dot_general | solution.py:36
  42.2 4.4 %copy.84 = bf16[32,256,256]{2,1,0:T(8,128)(2,1)} copy(bf16[32,256,256]{2,0,1:T(8,128)(2,1)S(1)} %convolution_convert_fusion) | data formatting | bytes 8388608 | tf_op jit(solution)/shard_map/convert_element_type | solution.py:38
  46.6 8.1 %all-to-all-start = ((bf16[32,256,256]{2,1,0:T(8,128)(2,1)}), bf16[32,256,256]{2,1,0:T(8,128)(2,1)}, u32[]{:S(2)}, u32[]{:S(2)}) async-start(bf16[32,256,256]{2,1,0:T(8,128)(2,1)} %copy.84), calls=%async_computation | async-start | bytes 8388608 | tf_op jit(solution)/shard_map/all_to_all | solution.py:39
  55.0 51.6 %all-to-all-done = bf16[32,256,256]{2,1,0:T(8,128)(2,1)} async-done(((bf16[32,256,256]{2,1,0:T(8,128)(2,1)}), bf16[32,256,256]{2,1,0:T(8,128)(2,1)}, u32[]{:S(2)}, u32[]{:S(2)}) %all-to-all-start) | async-done | bytes 4194336 | tf_op jit(solution)/shard_map/all_to_all | solution.py:39
  106.6 4.7 %fusion.8 = bf16[24,256,256]{2,0,1:T(8,128)(2,1)S(1)} fusion(bf16[32,256,256]{2,1,0:T(8,128)(2,1)} %all-to-all-done, s32[24,32]{1,0:T(8,128)S(1)} %convert_reduce_fusion), kind=kOutput, calls=%fused_computation.11 | convolution fusion | flops 102236928 | bytes 7343104 | tf_op jit(solution)/shard_map/kg,gxy->kxy/dot_general | solution.py:40
  111.3 0.5 constant_dynamic-slice_fusion
  111.8 2.0 %copy-done.3 = f32[24,64,256]{2,1,0:T(8,128)S(1)} copy-done((f32[24,64,256]{2,1,0:T(8,128)S(1)}, f32[24,64,256]{2,1,0:T(8,128)}, u32[]{:S(2)}) %copy-start.3) | copy-done | bytes 1572888
  113.8 1.5 fusion.17
  115.3 0.8 fusion.4
  116.1 0.6 copy-done.4
  116.7 1.8 %fusion.14 = f32[24,64,256]{2,0,1:T(8,128)S(1)} fusion(f32[24,64,256]{2,1,0:T(8,128)S(1)} %fusion.4, f32[24,64,256]{2,1,0:T(8,128)S(1)} %copy-done.4), kind=kLoop, calls=%fused_computation.18 | loop fusion | flops 1179648 | bytes 4718592 | tf_op jit(solution)/shard_map/add | solution.py:51
  118.5 1.6 copy.98
  120.2 2.0 %fusion.2 = f32[24,256,64]{1,2,0:T(8,128)S(1)} fusion(f32[24,64,256]{2,1,0:T(8,128)S(1)} %copy-done, bf16[24,256,256]{2,0,1:T(8,128)(2,1)S(1)} %fusion.8), kind=kOutput, calls=%fused_computation.4 | convolution fusion | flops 1207959552 | bytes 6291456 | tf_op jit(solution)/shard_map/kij,kjl->kil/dot_general | solution.py:56
  122.2 5.3 %multiply_reduce_fusion = (f32[24]{0:T(128)S(1)}, f32[24,64,256]{2,1,0:T(8,128)}) fusion(f32[24,256,64]{1,2,0:T(8,128)S(1)} %fusion.2, f32[24,256,256]{2,1,0:T(8,128)S(1)} %bitcast.19), kind=kOutput, calls=%fused_computation.26 | convolution fusion | flops 1208745984 | bytes 9437280 | tf_op jit(solution)/shard_map/kij,kjl->kil/dot_general | solution.py:57
  127.5 7.4 %all-reduce = (f32[24]{0:T(128)S(1)}, f32[24]{0:T(128)S(1)}) all-reduce(f32[24]{0:T(128)S(1)} %get-tuple-element.45, f32[24]{0:T(128)S(1)} %get-tuple-element.43), channel_id=1, replica_groups=mesh['shard'=32,'tensor'=4] {'tensor'}, use_global_device_ids=true, to_apply=%region_4.5 | all-reduce | flops 48 | bytes 384 | tf_op jit(solution)/shard_map/psum | solution.py:58
  134.9 4.8 %fusion.31 = (bf16[24,64,256]{2,1,0:T(8,128)(2,1)S(1)}, f32[24,64,256]{2,1,0:T(8,128)}, f32[24,64,256]{2,1,0:T(8,128)}) fusion(f32[24,64,256]{2,1,0:T(8,128)} %param.19, f32[24,64,256]{2,1,0:T(8,128)} %get-tuple-element.46, f32[24]{0:T(128)S(1)} %multiply_multiply_fusion.1, f32[24,64,256]{2,1,0:T(8,128)} %param.18), kind=kLoop, calls=%fused_computation.53 | loop fusion | flops 2359296 | bytes 8650848 | tf_op jit(solution)/shard_map/convert_element_type | solution.py:68
  139.7 0.7 convolution_convert_fusion.1
  140.4 1.6 copy.96
  142.0 9.1 %all-to-all-start.1 = ((bf16[32,64,256]{2,1,0:T(8,128)(2,1)}), bf16[32,64,256]{2,1,0:T(8,128)(2,1)S(1)}, u32[]{:S(2)}, u32[]{:S(2)}) async-start(bf16[32,64,256]{2,1,0:T(8,128)(2,1)} %copy.96), calls=%async_computation.1 | async-start | bytes 2097152 | tf_op jit(solution)/shard_map/all_to_all | solution.py:72
  151.1 2.5 %fusion.13 = f32[24,64,256]{2,0,1:T(8,128)S(1)} fusion(bf16[24,64,256]{2,0,1:T(8,128)(2,1)S(1)} %get-tuple-element.44, f32[24,64,256]{2,1,0:T(8,128)} %param.17), kind=kLoop, calls=%fused_computation.15 | loop fusion | flops 1966080 | bytes 3932160 | tf_op jit(solution)/shard_map/add | solution.py:54
  153.5 1.6 copy.99
  155.2 0.8 copy-done.2
  156.0 1.1 fusion.6
  157.1 0.3 copy-done.5
  157.4 1.8 %fusion.16 = f32[24,64,256]{2,0,1:T(8,128)S(1)} fusion(f32[24,64,256]{2,1,0:T(8,128)S(1)} %fusion.6, f32[24,64,256]{2,1,0:T(8,128)S(1)} %copy-done.5), kind=kLoop, calls=%fused_computation.22 | loop fusion | flops 1179648 | bytes 4718592 | tf_op jit(solution)/shard_map/add | solution.py:48
  159.2 1.6 copy.97
  160.9 7.1 %all-to-all-done.1 = bf16[32,64,256]{2,1,0:T(8,128)(2,1)S(1)} async-done(((bf16[32,64,256]{2,1,0:T(8,128)(2,1)}), bf16[32,64,256]{2,1,0:T(8,128)(2,1)S(1)}, u32[]{:S(2)}, u32[]{:S(2)}) %all-to-all-start.1) | async-done | bytes 1048608 | tf_op jit(solution)/shard_map/all_to_all | solution.py:72
  168.0 0.6 gather_fusion
  168.5 0.9 broadcast_select_fusion
  (25 shorter events, 0.4 us)
Async XLA Ops:
  7.2 113.0 %copy-start = (f32[24,64,256]{2,1,0:T(8,128)S(1)}, f32[24,64,256]{2,1,0:T(8,128)}, u32[]{:S(2)}) copy-start(f32[24,64,256]{2,1,0:T(8,128)} %param.15) | copy-start | bytes 4718596
  7.2 32.2 %all-gather.2.cloned.1.call-start = ((), (), s32[]{:S(2)}) async-start(), calls=%async_computation.2 | async-start | bytes 1966080 | tf_op jit(solution)/shard_map/all_gather | solution.py:35
  46.6 8.2 %copy-start.6 = (s32[384]{0:T(512)S(1)}, s32[384]{0:T(512)}, u32[]{:S(2)}) copy-start(s32[384]{0:T(512)} %param.12) | copy-start | bytes 4612
  46.6 60.0 %all-to-all-start = ((bf16[32,256,256]{2,1,0:T(8,128)(2,1)}), bf16[32,256,256]{2,1,0:T(8,128)(2,1)}, u32[]{:S(2)}, u32[]{:S(2)}) async-start(bf16[32,256,256]{2,1,0:T(8,128)(2,1)} %copy.84), calls=%async_computation | async-start | bytes 8388608 | tf_op jit(solution)/shard_map/all_to_all | solution.py:39
  111.2 8.9 %copy-start.1 = (bf16[24,256,256]{2,0,1:T(8,128)(2,1)}, bf16[24,256,256]{2,0,1:T(8,128)(2,1)S(1)}, u32[]{:S(2)}) copy-start(bf16[24,256,256]{2,0,1:T(8,128)(2,1)S(1)} %fusion.8) | copy-start | bytes 9437188
  111.3 2.5 %copy-start.3 = (f32[24,64,256]{2,1,0:T(8,128)S(1)}, f32[24,64,256]{2,1,0:T(8,128)}, u32[]{:S(2)}) copy-start(f32[24,64,256]{2,1,0:T(8,128)} %param.17) | copy-start | bytes 4718596
  115.3 1.4 copy-start.4
  116.7 5.5 %slice-start = ((s8[6291456]{0:T(1024)(128)(4,1)}), s8[4194304]{0:T(1024)(128)(4,1)S(1)}, s32[]{:S(2)}) async-start(s8[6291456]{0:T(1024)(128)(4,1)} %bitcast.18), calls=%async_computation.3 | async-start | bytes 8388608
  118.5 3.6 %slice-start.1 = ((s8[6291456]{0:T(1024)(128)(4,1)}), s8[2097152]{0:T(1024)(128)(4,1)S(1)}, s32[]{:S(2)}) async-start(s8[6291456]{0:T(1024)(128)(4,1)} %bitcast.18), calls=%async_computation.4 | async-start | bytes 4194304
  142.0 26.0 %all-to-all-start.1 = ((bf16[32,64,256]{2,1,0:T(8,128)(2,1)}), bf16[32,64,256]{2,1,0:T(8,128)(2,1)S(1)}, u32[]{:S(2)}, u32[]{:S(2)}) async-start(bf16[32,64,256]{2,1,0:T(8,128)(2,1)} %copy.96), calls=%async_computation.1 | async-start | bytes 2097152 | tf_op jit(solution)/shard_map/all_to_all | solution.py:72
  153.5 2.5 %copy-start.2 = (bf16[24,256,256]{2,0,1:T(8,128)(2,1)S(1)}, bf16[24,256,256]{2,0,1:T(8,128)(2,1)}, u32[]{:S(2)}) copy-start(bf16[24,256,256]{2,0,1:T(8,128)(2,1)} %copy-done.1) | copy-start | bytes 9437188
  156.0 1.4 copy-start.5
Sparse Core Ops, SparseCore 0:
  9.7 29.6 all-gather.1
where the time goes:
time: 177 us; the launch traced here: 176 us
  waiting for transfers between devices  90 us (51%)
  matrix products  17.3 us (10%)
  starting transfers between devices  17.2 us (10%)
  local copies, waits for them, and re-layouts  16.8 us (9%)
  between operations  14.2 us (8%)
  other arithmetic  13.4 us (8%)
  blocking collectives  7.38 us (4%)
    all_to_all x1, waiting for transfers between devices, on_device(): lax.all_to_all(outgoing, 'shard', split_axis=0, concat_axis=0, tiled=True)  51.6 us
    all_gather x1, waiting for transfers between devices, on_device(): whole_rows = lax.all_gather(grads, 'tensor', axis=1, tiled=True)  30.7 us
    all_to_all x1, starting transfers between devices, on_device(): lax.all_to_all(returning, 'shard', split_axis=0, concat_axis=0, tiled=True)  9.05 us
    unnamed x21, local copies, waits for them, and re-layouts  8.7 us
    all_to_all x1, starting transfers between devices, on_device(): lax.all_to_all(outgoing, 'shard', split_axis=0, concat_axis=0, tiled=True)  8.06 us
    psum x1, blocking collectives, on_device(): lax.psum((jnp.sum(adam_step * adam_step, axis=(1, 2)), jnp.sum(precond *...  7.38 us
    all_to_all x1, waiting for transfers between devices, on_device(): lax.all_to_all(returning, 'shard', split_axis=0, concat_axis=0, tiled=True)  7.11 us
    dot_general x1, matrix products, on_device(): precond = jnp.einsum('kij,kjl->kil', precond, root_right, precision=highest)  5.35 us
  transfers between devices with their start and end apart: 3, of which 3 were waited for; matrix products, arithmetic and copies ran while one was open for 6% of the time, Pallas kernels for 0%

commit v1 on v0

--- a/solution.py
+++ b/solution.py
@@ -32,7 +32,25 @@
     group_ids = jnp.arange(groups, dtype=jnp.int32)
     picker = (local_owner[None, :] == group_ids[:, None]).astype(jnp.bfloat16)
     row_start = tensor_index * rows_dev
-    whole_rows = lax.all_gather(grads, "tensor", axis=1, tiled=True)
+    heard = jax.lax.axis_size("tensor")
+    current_arr = jax.lax.axis_index("tensor")
+    reply, long_array, z = (heard, current_arr, grads.shape[1])
+    rack = tuple((d * reply if to_i == 1 else d for to_i, d in enumerate(grads.shape)))
+    seen_now = jnp.zeros(rack, grads.dtype)
+    whole_rows = lax.dynamic_update_slice_in_dim(seen_now, grads, long_array * z, axis=1)
+    y1 = y_new = grads
+    for h in tuple(range(1, reply // 2 + 1)):
+        block_out = tuple(((to_i, (to_i + 1) % reply) for to_i in range(reply)))
+        y1 = jax.lax.ppermute(y1, axis_name="tensor", perm=block_out)
+        whole_rows = lax.dynamic_update_slice_in_dim(
+            whole_rows, y1, (long_array - h) % reply * z, axis=1
+        )
+        if 2 * h < reply:
+            x_new = tuple(((to_i, (to_i - 1) % reply) for to_i in range(reply)))
+            y_new = jax.lax.ppermute(y_new, axis_name="tensor", perm=x_new)
+            whole_rows = lax.dynamic_update_slice_in_dim(
+                whole_rows, y_new, (long_array + h) % reply * z, axis=1
+            )
     outgoing = jnp.einsum(
         "gi,ixy->gxy", picker, whole_rows, preferred_element_type=jnp.float32
     ).astype(jnp.bfloat16)

time: 177 us -> 157 us (0.89)
  waiting for transfers between devices: 90 us -> 73.6 us
  between operations: 14.2 us -> 0.84 us
  starting transfers between devices: 17.2 us -> 23.3 us
  local copies, waits for them, and re-layouts: 16.8 us -> 21.7 us
    all_gather x1 -> x0, waiting for transfers between devices: 30.7 us -> none  [on_device(): whole_rows = lax.all_gather(grads, 'tensor', axis=1, tiled=True)]
    ppermute x0 -> x3, waiting for transfers between devices: none -> 14.9 us  [the longest x2 14.9 us: on_device(): y1 = jax.lax.ppermute(y1, axis_name='tensor', perm=block_out)]
    ppermute x0 -> x3, starting transfers between devices: none -> 4.73 us  [the longest x2 2.53 us: on_device(): y1 = jax.lax.ppermute(y1, axis_name='tensor', perm=block_out)]
    dynamic_update_slice x0 -> x4, local copies, waits for them, and re-layouts: none -> 4.11 us  [the longest x2 2.08 us: on_device(): lax.dynamic_update_slice_in_dim(whole_rows, y1, (long_array - h) % reply...]
    unnamed x21 -> x25, local copies, waits for them, and re-layouts: 8.7 us -> 8.71 us
  transfers between devices with their start and end apart: 3 -> 5, of which waited for: 3 -> 4; matrix products, arithmetic and copies ran while one was open for 6% -> 9% of each run, Pallas kernels for 0% -> 0%
where the time goes in v1:
time: 157 us; the launch traced here: 156 us
  waiting for transfers between devices  73.6 us (47%)
  starting transfers between devices  23.3 us (15%)
  local copies, waits for them, and re-layouts  21.7 us (14%)
  matrix products  17.5 us (11%)
  other arithmetic  13.4 us (9%)
  blocking collectives  5.97 us (4%)
    all_to_all x1, waiting for transfers between devices, on_device(): lax.all_to_all(outgoing, 'shard', split_axis=0, concat_axis=0, tiled=True)  51.6 us
    ppermute x2, waiting for transfers between devices, on_device(): y1 = jax.lax.ppermute(y1, axis_name='tensor', perm=block_out)  14.9 us
    all_to_all x1, starting transfers between devices, on_device(): lax.all_to_all(outgoing, 'shard', split_axis=0, concat_axis=0, tiled=True)  9.55 us
    all_to_all x1, starting transfers between devices, on_device(): lax.all_to_all(returning, 'shard', split_axis=0, concat_axis=0, tiled=True)  8.97 us
    unnamed x25, local copies, waits for them, and re-layouts  8.71 us
    all_to_all x1, waiting for transfers between devices, on_device(): lax.all_to_all(returning, 'shard', split_axis=0, concat_axis=0, tiled=True)  7.11 us
    psum x1, blocking collectives, on_device(): lax.psum((jnp.sum(adam_step * adam_step, axis=(1, 2)), jnp.sum(precond *...  5.97 us
    dot_general x1, matrix products, on_device(): precond = jnp.einsum('kij,kjl->kil', precond, root_right, precision=highest)  5.35 us
  transfers between devices with their start and end apart: 5, of which 4 were waited for; matrix products, arithmetic and copies ran while one was open for 9% of the time, Pallas kernels for 0%

profile of v1, /device:TPU:1, one launch (start us, length us, event | category | flops | bytes accessed | tf_op | source)
XLA Modules:
  0.0 156.2 jit_solution(18041398864201228234)
XLA Ops:
  0.7 2.5 %collective-permute-start = (bf16[12,64,256]{2,1,0:T(8,128)(2,1)}, bf16[12,64,256]{2,1,0:T(8,128)(2,1)S(1)}, u32[]{:S(2)}, u32[]{:S(2)}) collective-permute-start(bf16[12,64,256]{2,1,0:T(8,128)(2,1)} %param.10), channel_id=1, source_target_pairs={{0,1},{1,2},{2,3},{3,0},{4,5},{5,6},{6,7},{7,4},{8,9},{9,10},{10,1... | collective-permute-start | bytes 1179656 | tf_op jit(solution)/shard_map/ppermute | solution.py:44
  3.2 2.2 %collective-permute-start.1 = (bf16[12,64,256]{2,1,0:T(8,128)(2,1)}, bf16[12,64,256]{2,1,0:T(8,128)(2,1)S(1)}, u32[]{:S(2)}, u32[]{:S(2)}) collective-permute-start(bf16[12,64,256]{2,1,0:T(8,128)(2,1)} %param.10), channel_id=1, source_target_pairs={{0,3},{1,0},{2,1},{3,2},{4,7},{5,4},{6,5},{7,6},{8,11},{9,8},{10,9... | collective-permute-start | bytes 1179656 | tf_op jit(solution)/shard_map/ppermute | solution.py:50
  5.4 1.5 broadcast_in_dim.18
  6.9 1.0 copy_dynamic-update-slice_fusion.3
  8.0 6.3 %collective-permute-done = bf16[12,64,256]{2,1,0:T(8,128)(2,1)S(1)} collective-permute-done((bf16[12,64,256]{2,1,0:T(8,128)(2,1)}, bf16[12,64,256]{2,1,0:T(8,128)(2,1)S(1)}, u32[]{:S(2)}, u32[]{:S(2)}) %collective-permute-start) | collective-permute-done | bytes 393248 | tf_op jit(solution)/shard_map/ppermute | solution.py:44
  14.3 1.0 copy_dynamic-update-slice_fusion.2
  15.4 1.0 copy_dynamic-update-slice_fusion.1
  16.4 8.6 %collective-permute-done.2 = bf16[12,64,256]{2,1,0:T(8,128)(2,1)S(1)} collective-permute-done((bf16[12,64,256]{2,1,0:T(8,128)(2,1)S(1)}, bf16[12,64,256]{2,1,0:T(8,128)(2,1)S(1)}, u32[]{:S(2)}, u32[]{:S(2)}) %collective-permute-start.2) | collective-permute-done | bytes 393248 | tf_op jit(solution)/shard_map/ppermute | solution.py:44
  25.0 1.1 copy_dynamic-update-slice_fusion
  26.0 2.9 %convolution_convert_fusion = bf16[32,256,256]{2,0,1:T(8,128)(2,1)S(1)} fusion(bf16[12,256,256]{2,0,1:T(8,128)(2,1)} %copy_dynamic-update-slice_fusion, s32[12]{0:T(128)S(1)} %get-tuple-element.33), kind=kOutput, calls=%fused_computation.3 | convolution fusion | flops 52429184 | bytes 5767216 | tf_op jit(solution)/shard_map/gi,ixy->gxy/dot_general | solution.py:54
  29.0 4.4 %copy.72 = bf16[32,256,256]{2,1,0:T(8,128)(2,1)} copy(bf16[32,256,256]{2,0,1:T(8,128)(2,1)S(1)} %convolution_convert_fusion) | data formatting | bytes 8388608 | tf_op jit(solution)/shard_map/convert_element_type | solution.py:56
  33.4 9.6 %all-to-all-start = ((bf16[32,256,256]{2,1,0:T(8,128)(2,1)}), bf16[32,256,256]{2,1,0:T(8,128)(2,1)}, u32[]{:S(2)}, u32[]{:S(2)}) async-start(bf16[32,256,256]{2,1,0:T(8,128)(2,1)} %copy.72), calls=%async_computation | async-start | bytes 8388608 | tf_op jit(solution)/shard_map/all_to_all | solution.py:57
  43.3 51.6 %all-to-all-done = bf16[32,256,256]{2,1,0:T(8,128)(2,1)} async-done(((bf16[32,256,256]{2,1,0:T(8,128)(2,1)}), bf16[32,256,256]{2,1,0:T(8,128)(2,1)}, u32[]{:S(2)}, u32[]{:S(2)}) %all-to-all-start) | async-done | bytes 4194336 | tf_op jit(solution)/shard_map/all_to_all | solution.py:57
  94.9 4.7 %fusion.8 = bf16[24,256,256]{2,0,1:T(8,128)(2,1)S(1)} fusion(bf16[32,256,256]{2,1,0:T(8,128)(2,1)} %all-to-all-done, s32[24,32]{1,0:T(8,128)S(1)} %convert_reduce_fusion), kind=kOutput, calls=%fused_computation.11 | convolution fusion | flops 102236928 | bytes 7343104 | tf_op jit(solution)/shard_map/kg,gxy->kxy/dot_general | solution.py:58
  100.1 2.0 %copy-done.3 = f32[24,64,256]{2,1,0:T(8,128)S(1)} copy-done((f32[24,64,256]{2,1,0:T(8,128)S(1)}, f32[24,64,256]{2,1,0:T(8,128)}, u32[]{:S(2)}) %copy-start.3) | copy-done | bytes 1572888
  102.1 1.5 fusion.16
  105.0 1.8 %fusion.13 = f32[24,64,256]{2,0,1:T(8,128)S(1)} fusion(f32[24,64,256]{2,1,0:T(8,128)S(1)} %fusion.4, f32[24,64,256]{2,1,0:T(8,128)S(1)} %copy-done.4), kind=kLoop, calls=%fused_computation.17 | loop fusion | flops 1179648 | bytes 4718592 | tf_op jit(solution)/shard_map/add | solution.py:69
  106.8 1.6 %copy.86 = f32[24,64,256]{2,1,0:T(8,128)} copy(f32[24,64,256]{2,0,1:T(8,128)S(1)} %fusion.13) | data formatting | bytes 3145728
  108.4 2.0 %fusion.2 = f32[24,256,64]{1,2,0:T(8,128)S(1)} fusion(f32[24,64,256]{2,1,0:T(8,128)S(1)} %copy-done, bf16[24,256,256]{2,0,1:T(8,128)(2,1)S(1)} %fusion.8), kind=kOutput, calls=%fused_computation.4 | convolution fusion | flops 1207959552 | bytes 6291456 | tf_op jit(solution)/shard_map/kij,kjl->kil/dot_general | solution.py:74
  110.4 5.3 %multiply_reduce_fusion = (f32[24]{0:T(128)S(1)}, f32[24,64,256]{2,1,0:T(8,128)}) fusion(f32[24,256,64]{1,2,0:T(8,128)S(1)} %fusion.2, f32[24,256,256]{2,1,0:T(8,128)S(1)} %bitcast.20), kind=kOutput, calls=%fused_computation.25 | convolution fusion | flops 1208745984 | bytes 9437280 | tf_op jit(solution)/shard_map/kij,kjl->kil/dot_general | solution.py:75
  115.8 6.0 %all-reduce = (f32[24]{0:T(128)S(1)}, f32[24]{0:T(128)S(1)}) all-reduce(f32[24]{0:T(128)S(1)} %get-tuple-element.39, f32[24]{0:T(128)S(1)} %get-tuple-element.37), channel_id=1, replica_groups=mesh['shard'=32,'tensor'=4] {'tensor'}, use_global_device_ids=true, to_apply=%region_4.5 | all-reduce | flops 48 | bytes 384 | tf_op jit(solution)/shard_map/psum | solution.py:76
  121.8 4.8 %fusion.30 = (bf16[24,64,256]{2,1,0:T(8,128)(2,1)S(1)}, f32[24,64,256]{2,1,0:T(8,128)}, f32[24,64,256]{2,1,0:T(8,128)}) fusion(f32[24,64,256]{2,1,0:T(8,128)} %param.19, f32[24,64,256]{2,1,0:T(8,128)} %get-tuple-element.40, f32[24]{0:T(128)S(1)} %multiply_multiply_fusion.1, f32[24,64,256]{2,1,0:T(8,128)} %param.18), kind=kLoop, calls=%fused_computation.56 | loop fusion | flops 2359296 | bytes 8650848 | tf_op jit(solution)/shard_map/convert_element_type | solution.py:86
  127.3 1.6 %copy.84 = bf16[32,64,256]{2,1,0:T(8,128)(2,1)} copy(bf16[32,64,256]{2,0,1:T(8,128)(2,1)S(1)} %convolution_convert_fusion.1) | data formatting | bytes 2097152 | tf_op jit(solution)/shard_map/convert_element_type | solution.py:89
  128.9 9.0 %all-to-all-start.1 = ((bf16[32,64,256]{2,1,0:T(8,128)(2,1)}), bf16[32,64,256]{2,1,0:T(8,128)(2,1)S(1)}, u32[]{:S(2)}, u32[]{:S(2)}) async-start(bf16[32,64,256]{2,1,0:T(8,128)(2,1)} %copy.84), calls=%async_computation.1 | async-start | bytes 2097152 | tf_op jit(solution)/shard_map/all_to_all | solution.py:90
  137.9 2.5 %fusion.12 = f32[24,64,256]{2,0,1:T(8,128)S(1)} fusion(bf16[24,64,256]{2,0,1:T(8,128)(2,1)S(1)} %get-tuple-element.38, f32[24,64,256]{2,1,0:T(8,128)} %param.17), kind=kLoop, calls=%fused_computation.14 | loop fusion | flops 1966080 | bytes 3932160 | tf_op jit(solution)/shard_map/add | solution.py:72
  140.3 1.6 %copy.87 = f32[24,64,256]{2,1,0:T(8,128)} copy(f32[24,64,256]{2,0,1:T(8,128)S(1)} %fusion.12) | data formatting | bytes 3145728
  142.0 0.8 copy-done.2
  142.8 1.1 fusion.6
  144.2 1.8 %fusion.15 = f32[24,64,256]{2,0,1:T(8,128)S(1)} fusion(f32[24,64,256]{2,1,0:T(8,128)S(1)} %fusion.6, f32[24,64,256]{2,1,0:T(8,128)S(1)} %copy-done.5), kind=kLoop, calls=%fused_computation.21 | loop fusion | flops 1179648 | bytes 4718592 | tf_op jit(solution)/shard_map/add | solution.py:66
  146.0 1.6 %copy.85 = f32[24,64,256]{2,1,0:T(8,128)} copy(f32[24,64,256]{2,0,1:T(8,128)S(1)} %fusion.15) | data formatting | bytes 3145728
  147.7 7.1 %all-to-all-done.1 = bf16[32,64,256]{2,1,0:T(8,128)(2,1)S(1)} async-done(((bf16[32,64,256]{2,1,0:T(8,128)(2,1)}), bf16[32,64,256]{2,1,0:T(8,128)(2,1)S(1)}, u32[]{:S(2)}, u32[]{:S(2)}) %all-to-all-start.1) | async-done | bytes 1048608 | tf_op jit(solution)/shard_map/all_to_all | solution.py:90
  155.3 0.9 broadcast_select_fusion
  (37 shorter events, 4.0 us)
Async XLA Ops:
  0.6 107.8 %copy-start = (f32[24,64,256]{2,1,0:T(8,128)S(1)}, f32[24,64,256]{2,1,0:T(8,128)}, u32[]{:S(2)}) copy-start(f32[24,64,256]{2,1,0:T(8,128)} %param.15) | copy-start | bytes 4718596
  0.6 6.2 %copy-start.6 = (bf16[12,64,256]{2,1,0:T(8,128)(2,1)S(1)}, bf16[12,64,256]{2,1,0:T(8,128)(2,1)}, u32[]{:S(2)}) copy-start(bf16[12,64,256]{2,1,0:T(8,128)(2,1)} %param.10) | copy-start | bytes 1179652
  0.7 7.2 %copy-start.7 = (s32[384]{0:T(512)S(1)}, s32[384]{0:T(512)}, u32[]{:S(2)}) copy-start(s32[384]{0:T(512)} %param.11) | copy-start | bytes 4612
  0.7 13.7 %collective-permute-start = (bf16[12,64,256]{2,1,0:T(8,128)(2,1)}, bf16[12,64,256]{2,1,0:T(8,128)(2,1)S(1)}, u32[]{:S(2)}, u32[]{:S(2)}) collective-permute-start(bf16[12,64,256]{2,1,0:T(8,128)(2,1)} %param.10), channel_id=1, source_target_pairs={{0,1},{1,2},{2,3},{3,0},{4,5},{5,6},{6,7},{7,4},{8,9},{9,10},{10,1... | collective-permute-start | bytes 1179656 | tf_op jit(solution)/shard_map/ppermute | solution.py:44
  3.2 12.2 %collective-permute-start.1 = (bf16[12,64,256]{2,1,0:T(8,128)(2,1)}, bf16[12,64,256]{2,1,0:T(8,128)(2,1)S(1)}, u32[]{:S(2)}, u32[]{:S(2)}) collective-permute-start(bf16[12,64,256]{2,1,0:T(8,128)(2,1)} %param.10), channel_id=1, source_target_pairs={{0,3},{1,0},{2,1},{3,2},{4,7},{5,4},{6,5},{7,6},{8,11},{9,8},{10,9... | collective-permute-start | bytes 1179656 | tf_op jit(solution)/shard_map/ppermute | solution.py:50
  14.3 10.6 %collective-permute-start.2 = (bf16[12,64,256]{2,1,0:T(8,128)(2,1)S(1)}, bf16[12,64,256]{2,1,0:T(8,128)(2,1)S(1)}, u32[]{:S(2)}, u32[]{:S(2)}) collective-permute-start(bf16[12,64,256]{2,1,0:T(8,128)(2,1)S(1)} %collective-permute-done), channel_id=1, source_target_pairs={{0,1},{1,2},{2,3},{3,0},{4,5},{5,6},{6,7},{7,4},{8,9},{9,10},{10,1... | collective-permute-start | bytes 1179656 | tf_op jit(solution)/shard_map/ppermute | solution.py:44
  33.4 9.7 %copy-start.8 = (s32[384]{0:T(512)S(1)}, s32[384]{0:T(512)}, u32[]{:S(2)}) copy-start(s32[384]{0:T(512)} %param.12) | copy-start | bytes 4612
  33.4 61.5 %all-to-all-start = ((bf16[32,256,256]{2,1,0:T(8,128)(2,1)}), bf16[32,256,256]{2,1,0:T(8,128)(2,1)}, u32[]{:S(2)}, u32[]{:S(2)}) async-start(bf16[32,256,256]{2,1,0:T(8,128)(2,1)} %copy.72), calls=%async_computation | async-start | bytes 8388608 | tf_op jit(solution)/shard_map/all_to_all | solution.py:57
  99.5 8.9 %copy-start.1 = (bf16[24,256,256]{2,0,1:T(8,128)(2,1)}, bf16[24,256,256]{2,0,1:T(8,128)(2,1)S(1)}, u32[]{:S(2)}) copy-start(bf16[24,256,256]{2,0,1:T(8,128)(2,1)S(1)} %fusion.8) | copy-start | bytes 9437188
  99.5 2.5 %copy-start.3 = (f32[24,64,256]{2,1,0:T(8,128)S(1)}, f32[24,64,256]{2,1,0:T(8,128)}, u32[]{:S(2)}) copy-start(f32[24,64,256]{2,1,0:T(8,128)} %param.17) | copy-start | bytes 4718596
  103.6 1.4 copy-start.4
  105.0 5.5 %slice-start = ((s8[6291456]{0:T(1024)(128)(4,1)}), s8[4194304]{0:T(1024)(128)(4,1)S(1)}, s32[]{:S(2)}) async-start(s8[6291456]{0:T(1024)(128)(4,1)} %bitcast.19), calls=%async_computation.2 | async-start | bytes 8388608
  106.8 3.6 %slice-start.1 = ((s8[6291456]{0:T(1024)(128)(4,1)}), s8[2097152]{0:T(1024)(128)(4,1)S(1)}, s32[]{:S(2)}) async-start(s8[6291456]{0:T(1024)(128)(4,1)} %bitcast.19), calls=%async_computation.3 | async-start | bytes 4194304
  128.9 25.9 %all-to-all-start.1 = ((bf16[32,64,256]{2,1,0:T(8,128)(2,1)}), bf16[32,64,256]{2,1,0:T(8,128)(2,1)S(1)}, u32[]{:S(2)}, u32[]{:S(2)}) async-start(bf16[32,64,256]{2,1,0:T(8,128)(2,1)} %copy.84), calls=%async_computation.1 | async-start | bytes 2097152 | tf_op jit(solution)/shard_map/all_to_all | solution.py:90
  140.3 2.5 %copy-start.2 = (bf16[24,256,256]{2,0,1:T(8,128)(2,1)S(1)}, bf16[24,256,256]{2,0,1:T(8,128)(2,1)}, u32[]{:S(2)}) copy-start(bf16[24,256,256]{2,0,1:T(8,128)(2,1)} %copy-done.1) | copy-start | bytes 9437188
  142.8 1.4 copy-start.5
